TPU v7x, 32 devices: a whole 2x2x4 slice. The times are simulated.
32 devices in a mesh: node: 8 (over z, x), feat: 4 (over y, core).
Axes of the slice: x: 2, y: 2, z: 4, core: 2. Of those that a mesh axis runs over, the one named last changes fastest.
Arguments:
- features: bfloat16 [128, 128, 128], P('node', 'feat'), may hold values from -6 to 6
- tile_values: bfloat16 [2048, 128, 128], P('node'), may hold values from -0.125 to 0.125
- tile_row: int32 [2048], P('node'), may hold values from 0 to 127, as said below
- tile_col: int32 [2048], P('node'), may hold values from 0 to 127, as said below
- tile_count: int32 [8], P('node'), may hold values from 32 to 256, as said below
- weight: float32 [128, 128], P('feat'), may hold values from -0.5 to 0.5
- first_moment: float32 [128, 128], P('feat'), may hold values from -3 to 3
- second_moment: float32 [128, 128], P('feat'), may hold values from 0.1 to 2
- cotangent: bfloat16 [128, 128, 128], P('node', 'feat'), may hold values from -6 to 6
Outputs:
- activated: bfloat16 [128, 128, 128], P('node', 'feat')
- feature_grad: float32 [128, 128, 128], P('node', 'feat')
- new_weight: float32 [128, 128], P('feat')
- new_first: float32 [128, 128], P('feat')
- new_second: float32 [128, 128], P('feat')
Inputs may be any that keep to these rules, and one draw needn't show every extreme that they name: `tile_row`: the slots of index d of node (slots d * 256 to (d + 1) * 256 - 1) name target blocks of that index only: d * 16 to (d + 1) * 16 - 1. `tile_col`: A slot's source block lies on an index of node at most 2 away from the slot's own index around the closed loop of node indices; both distances 2 occur on every index. `tile_count`: some index of node has all 256 slots live, some has 32.
All inputs are finite; a program needn't handle non-finite values.
Results may differ from a plain program's by a relative error of at most 0.0058.
Values may be sent and summed in bfloat16 or wider, within the bound.
No kernel may reach another device: no remote copies, remote signals or barrier semaphores. Data moves between devices by JAX's collectives and lax.ppermute only.
A program may use at most 64 MiB of HBM per device.

v0:
```python
import math
import jax
import jax.numpy as jnp
from jax import lax
from jax.sharding import PartitionSpec as P

REACH = 2
first_decay = 0.9
second_decay = 0.999
learn_rate = 0.05
first_fix = 1.0 - 0.9**10
second_fix = 1.0 - 0.999**10
adam_eps = 1e-08


def passed_along(block, axis, distance):
    devices = range(lax.axis_size(axis))
    route = [((i - distance) % len(devices), i) for i in devices]
    return lax.ppermute(block, axis, route)


def elu_slope(preact):
    return jnp.where(preact > 0, 1.0, jnp.exp(jnp.minimum(preact, 0.0)))


def one_hot_table(indices, count, dtype):
    return (indices[:, None] == jnp.arange(count)[None, :]).astype(dtype)


def per_device(
    features,
    tile_values,
    tile_row,
    tile_col,
    tile_count,
    weight,
    first_moment,
    second_moment,
    cotangent,
):
    cycle_size = lax.axis_size("node")
    own_node = lax.axis_index("node")
    blocks = features.shape[0]
    width_local = features.shape[1]
    tile_size = features.shape[2]
    slots = tile_values.shape[0]
    live = (jnp.arange(slots) < tile_count[0]).astype(jnp.float32)
    local_row = tile_row - own_node * blocks
    col_owner = tile_col // blocks
    col_block = tile_col % blocks
    offset = (col_owner - own_node) % cycle_size
    offset = jnp.where(offset > cycle_size // 2, offset - cycle_size, offset)
    source_slot = (offset + REACH) * blocks + col_block
    targets = (2 * REACH + 1) * blocks
    pick_source = one_hot_table(source_slot, targets, jnp.bfloat16)
    pick_row = one_hot_table(local_row, blocks, jnp.bfloat16)
    add_row = one_hot_table(local_row, blocks, jnp.float32) * live[:, None]
    add_source = one_hot_table(source_slot, targets, jnp.float32) * live[:, None]
    pieces = []
    for distance in range(-REACH, REACH + 1):
        if distance == 0:
            pieces.append(features)
        else:
            pieces.append(passed_along(features, "node", -distance))
    nearby = jnp.concatenate(pieces, axis=0)
    sources = jnp.einsum(
        "ts,sfk->tfk", pick_source, nearby, preferred_element_type=jnp.float32
    ).astype(jnp.bfloat16)
    forward_terms = jnp.einsum(
        "tfk,tjk->tfj", sources, tile_values, preferred_element_type=jnp.float32
    )
    aggregate = jnp.einsum("tb,tfj->bfj", add_row, forward_terms, precision=lax.Precision.HIGHEST)
    aggregate = aggregate.astype(jnp.bfloat16)
    weight_half = weight.astype(jnp.bfloat16)
    aggregate_all, weight_all = (
        lax.all_gather(aggregate, "feat", axis=1, tiled=True),
        lax.all_gather(weight_half, "feat", axis=0, tiled=True),
    )
    column_start = lax.axis_index("feat") * width_local
    weight_cols = lax.dynamic_slice_in_dim(weight_all, column_start, width_local, 1)
    preact = jnp.einsum(
        "bij,io->boj", aggregate_all, weight_cols, preferred_element_type=jnp.float32
    )
    activated = jax.nn.elu(preact).astype(jnp.bfloat16)
    slope_grad = (cotangent.astype(jnp.float32) * elu_slope(preact)).astype(jnp.bfloat16)
    slope_all = lax.all_gather(slope_grad, "feat", axis=1, tiled=True)
    node_total = cycle_size * blocks * tile_size
    grad_local = jnp.einsum("bij,boj->io", aggregate, slope_all, preferred_element_type=jnp.float32)
    grad = lax.psum(grad_local, "node") * (1.0 / math.sqrt(node_total))
    back_rows = jnp.einsum(
        "io,boj->bij", weight_half, slope_all, preferred_element_type=jnp.float32
    ).astype(jnp.bfloat16)
    back_sources = jnp.einsum(
        "tb,bfj->tfj", pick_row, back_rows, preferred_element_type=jnp.float32
    ).astype(jnp.bfloat16)
    back_terms = jnp.einsum(
        "tfj,tjk->tfk", back_sources, tile_values, preferred_element_type=jnp.float32
    )
    outgoing = jnp.einsum("ts,tfk->sfk", add_source, back_terms, precision=lax.Precision.HIGHEST)
    outgoing = outgoing.reshape(2 * REACH + 1, blocks, width_local, tile_size)
    feature_grad = outgoing[REACH]
    for distance in range(-REACH, REACH + 1):
        if distance != 0:
            feature_grad = feature_grad + passed_along(outgoing[distance + REACH], "node", distance)
    new_first = first_decay * first_moment + (1.0 - first_decay) * grad
    new_second = second_decay * second_moment + (1.0 - second_decay) * grad * grad
    new_weight = weight - learn_rate * (new_first / first_fix) / (
        jnp.sqrt(new_second / second_fix) + adam_eps
    )
    return (activated, feature_grad, new_weight, new_first, new_second)


def solution(mesh):
    return jax.shard_map(
        per_device,
        mesh=mesh,
        in_specs=(
            P("node", "feat", None),
            P("node", None, None),
            P("node"),
            P("node"),
            P("node"),
            P("feat", None),
            P("feat", None),
            P("feat", None),
            P("node", "feat", None),
        ),
        out_specs=(
            P("node", "feat", None),
            P("node", "feat", None),
            P("feat", None),
            P("feat", None),
            P("feat", None),
        ),
        check_vma=False,
    )
```

profile of v0, /device:TPU:0, one launch (start us, length us, event | category | flops | bytes accessed | tf_op | source)
XLA Modules:
  0.0 112.7 jit_solution(17020929460422994571)
XLA Ops:
  0.6 6.0 %collective-permute-start.2 = (bf16[16,32,128]{2,1,0:T(8,128)(2,1)}, bf16[16,32,128]{2,1,0:T(8,128)(2,1)S(1)}, u32[]{:S(2)}, u32[]{:S(2)}) collective-permute-start(bf16[16,32,128]{2,1,0:T(8,128)(2,1)} %param.9), channel_id=1, source_target_pairs={{4,0},{8,4},{12,8},{16,12},{20,16},{24,20},{28,24},{0,28},{5,1},{9... | collective-permute-start | bytes 393224 | tf_op jit(solution)/shard_map/ppermute | solution.py:19
  6.7 0.0 collective-permute-start.1
  6.7 3.8 %collective-permute-start.3 = (bf16[16,32,128]{2,1,0:T(8,128)(2,1)}, bf16[16,32,128]{2,1,0:T(8,128)(2,1)S(1)}, u32[]{:S(2)}, u32[]{:S(2)}) collective-permute-start(bf16[16,32,128]{2,1,0:T(8,128)(2,1)} %param.9), channel_id=1, source_target_pairs={{8,0},{12,4},{16,8},{20,12},{24,16},{28,20},{0,24},{4,28},{9,1},{1... | collective-permute-start | bytes 393224 | tf_op jit(solution)/shard_map/ppermute | solution.py:19
  10.5 0.7 fusion.41
  11.2 0.7 broadcast_subtract_fusion
  12.5 0.7 convert_element_type.38
  13.3 5.2 %all_gather.9 = bf16[128,128]{1,0:T(8,128)(2,1)S(1)} all-gather(bf16[32,128]{1,0:T(8,128)(2,1)S(1)} %convert_element_type.38), channel_id=1, replica_groups=mesh['node'=8,'feat'=4] {'feat'}, dimensions={0}, use_global_device_ids=true | all-gather | bytes 40960 | tf_op jit(solution)/shard_map/all_gather | solution.py:77
  18.4 0.0 collective-permute-done
  18.5 0.0 collective-permute-done.1
  18.5 0.9 constant_dynamic-update-slice_fusion.2
  19.5 0.8 fusion.10
  20.3 7.2 %fusion.4 = f32[256,32,128]{2,1,0:T(8,128)S(1)} fusion(bf16[256,128,128]{2,1,0:T(8,128)(2,1)} %param.10, bf16[256,32,128]{2,0,1:T(8,128)(2,1)S(1)} %fusion.10), kind=kOutput, calls=%fused_computation.6 | convolution fusion | flops 268435456 | bytes 14680064 | tf_op jit(solution)/shard_map/tfk,tjk->tfj/dot_general | solution.py:69
  27.5 4.4 %fusion.7 = bf16[16,32,128]{2,0,1:T(8,128)(2,1)S(1)} fusion(f32[256,32,128]{2,1,0:T(8,128)S(1)} %fusion.4, f32[256]{0:T(256)S(1)} %compare_convert_fusion, s32[256]{0:T(256)S(1)} %broadcast_subtract_fusion), kind=kOutput, calls=%fused_computation.11 | convolution fusion | flops 201400320 | bytes 4327424 | tf_op jit(solution)/shard_map/tb,tfj->bfj/dot_general | solution.py:72
  31.9 7.3 %all_gather.10 = bf16[16,128,128]{2,0,1:T(8,128)(2,1)S(1)} all-gather(bf16[16,32,128]{2,0,1:T(8,128)(2,1)S(1)} %fusion.7), channel_id=1, replica_groups=mesh['node'=8,'feat'=4] {'feat'}, dimensions={1}, use_global_device_ids=true | all-gather | bytes 655360 | tf_op jit(solution)/shard_map/all_gather | solution.py:76
  39.1 1.1 fusion.16
  40.2 7.5 %all_gather.11 = bf16[16,128,128]{2,1,0:T(8,128)(2,1)S(1)} all-gather(bf16[16,32,128]{2,1,0:T(8,128)(2,1)S(1)} %get-tuple-element.22), channel_id=1, replica_groups=mesh['node'=8,'feat'=4] {'feat'}, dimensions={1}, use_global_device_ids=true | all-gather | bytes 655360 | tf_op jit(solution)/shard_map/all_gather | solution.py:86
  47.7 0.3 fusion.6
  48.0 0.2 copy.25
  48.3 0.7 fusion.34
  49.0 7.2 %fusion.5 = f32[256,32,128]{2,1,0:T(8,128)S(1)} fusion(bf16[256,128,128]{2,1,0:T(8,128)(2,1)} %param.10, bf16[256,32,128]{2,0,1:T(8,128)(2,1)S(1)} %fusion.34), kind=kOutput, calls=%fused_computation.7 | convolution fusion | flops 268435456 | bytes 14680064 | tf_op jit(solution)/shard_map/tfj,tjk->tfk/dot_general | solution.py:96
  56.2 4.9 %fusion = f32[80,32,128]{2,0,1:T(8,128)S(1)} fusion(f32[256,32,128]{2,1,0:T(8,128)S(1)} %fusion.5, f32[256]{0:T(256)S(1)} %compare_convert_fusion, s32[256]{0:T(256)S(1)} %fusion.41), kind=kOutput, calls=%fused_computation | convolution fusion | flops 1006673920 | bytes 5507072 | tf_op jit(solution)/shard_map/ts,tfk->sfk/dot_general | solution.py:99
  61.1 0.9 fusion.48
  62.0 0.0 collective-permute-start.4
  62.0 2.0 %collective-permute-start.7 = (f32[16,32,128]{2,0,1:T(8,128)}, f32[16,32,128]{2,0,1:T(8,128)S(1)}, u32[]{:S(2)}, u32[]{:S(2)}) collective-permute-start(f32[16,32,128]{2,0,1:T(8,128)} %get-tuple-element.19), channel_id=1, source_target_pairs={{24,0},{28,4},{0,8},{4,12},{8,16},{12,20},{16,24},{20,28},{25,1},{... | collective-permute-start | bytes 786440 | tf_op jit(solution)/shard_map/ppermute | solution.py:19
  64.0 1.5 %collective-permute-start.6 = (f32[16,32,128]{2,0,1:T(8,128)S(1)}, f32[16,32,128]{2,0,1:T(8,128)S(1)}, u32[]{:S(2)}, u32[]{:S(2)}) collective-permute-start(f32[16,32,128]{2,0,1:T(8,128)S(1)} %get-tuple-element.20), channel_id=1, source_target_pairs={{28,0},{0,4},{4,8},{8,12},{12,16},{16,20},{20,24},{24,28},{29,1},{... | collective-permute-start | bytes 786440 | tf_op jit(solution)/shard_map/ppermute | solution.py:19
  65.5 3.3 %collective-permute-start.5 = (f32[16,32,128]{2,0,1:T(8,128)S(1)}, f32[16,32,128]{2,0,1:T(8,128)S(1)}, u32[]{:S(2)}, u32[]{:S(2)}) collective-permute-start(f32[16,32,128]{2,0,1:T(8,128)S(1)} %get-tuple-element.21), channel_id=1, source_target_pairs={{4,0},{8,4},{12,8},{16,12},{20,16},{24,20},{28,24},{0,28},{5,1},{9... | collective-permute-start | bytes 786440 | tf_op jit(solution)/shard_map/ppermute | solution.py:19
  68.8 0.9 convolution_bitcast_fusion.1
  69.7 40.8 %psum.7 = f32[32,128]{1,0:T(8,128)S(1)} all-reduce(f32[32,128]{1,0:T(8,128)} %convolution_bitcast_fusion.1), channel_id=1, replica_groups=mesh['node'=8,'feat'=4] {'node'}, use_global_device_ids=true, to_apply=%region_0.1 | all-reduce | flops 4096 | bytes 32768 | tf_op jit(solution)/shard_map/psum | solution.py:89
  110.4 1.4 %divide_subtract_fusion = (f32[32,128]{1,0:T(8,128)}, f32[32,128]{1,0:T(8,128)}, f32[32,128]{1,0:T(8,128)}) fusion(f32[32,128]{1,0:T(8,128)S(1)} %copy-done, f32[32,128]{1,0:T(8,128)S(1)} %psum.7, f32[32,128]{1,0:T(8,128)} %param.15, f32[32,128]{1,0:T(8,128)} %param.16), kind=kLoop, calls=%fused_computation.39 | loop fusion | flops 53248 | bytes 114688 | tf_op jit(solution)/shard_map/sub | solution.py:107
  111.8 0.0 collective-permute-done.4
  111.8 0.1 fusion.19
  111.9 0.8 copy.21
  (15 shorter events, 0.1 us)
Async XLA Ops:
  0.6 18.8 %collective-permute-start.2 = (bf16[16,32,128]{2,1,0:T(8,128)(2,1)}, bf16[16,32,128]{2,1,0:T(8,128)(2,1)S(1)}, u32[]{:S(2)}, u32[]{:S(2)}) collective-permute-start(bf16[16,32,128]{2,1,0:T(8,128)(2,1)} %param.9), channel_id=1, source_target_pairs={{4,0},{8,4},{12,8},{16,12},{20,16},{24,20},{28,24},{0,28},{5,1},{9... | collective-permute-start | bytes 393224 | tf_op jit(solution)/shard_map/ppermute | solution.py:19
  6.7 11.8 %collective-permute-start.1 = (bf16[16,32,128]{2,1,0:T(8,128)(2,1)}, bf16[16,32,128]{2,1,0:T(8,128)(2,1)S(1)}, u32[]{:S(2)}, u32[]{:S(2)}) collective-permute-start(bf16[16,32,128]{2,1,0:T(8,128)(2,1)} %param.9), channel_id=1, source_target_pairs={{28,0},{0,4},{4,8},{8,12},{12,16},{16,20},{20,24},{24,28},{29,1},{... | collective-permute-start | bytes 393224 | tf_op jit(solution)/shard_map/ppermute | solution.py:19
  6.7 11.8 %collective-permute-start = (bf16[16,32,128]{2,1,0:T(8,128)(2,1)}, bf16[16,32,128]{2,1,0:T(8,128)(2,1)S(1)}, u32[]{:S(2)}, u32[]{:S(2)}) collective-permute-start(bf16[16,32,128]{2,1,0:T(8,128)(2,1)} %param.9), channel_id=1, source_target_pairs={{24,0},{28,4},{0,8},{4,12},{8,16},{12,20},{16,24},{20,28},{25,1},{... | collective-permute-start | bytes 393224 | tf_op jit(solution)/shard_map/ppermute | solution.py:19
  6.7 12.8 %collective-permute-start.3 = (bf16[16,32,128]{2,1,0:T(8,128)(2,1)}, bf16[16,32,128]{2,1,0:T(8,128)(2,1)S(1)}, u32[]{:S(2)}, u32[]{:S(2)}) collective-permute-start(bf16[16,32,128]{2,1,0:T(8,128)(2,1)} %param.9), channel_id=1, source_target_pairs={{8,0},{12,4},{16,8},{20,12},{24,16},{28,20},{0,24},{4,28},{9,1},{1... | collective-permute-start | bytes 393224 | tf_op jit(solution)/shard_map/ppermute | solution.py:19
  27.5 11.6 %copy-start.1 = (bf16[16,32,128]{2,1,0:T(8,128)(2,1)S(1)}, bf16[16,32,128]{2,1,0:T(8,128)(2,1)}, u32[]{:S(2)}) copy-start(bf16[16,32,128]{2,1,0:T(8,128)(2,1)} %param.17) | copy-start | bytes 393220
  56.2 54.2 %copy-start = (f32[32,128]{1,0:T(8,128)S(1)}, f32[32,128]{1,0:T(8,128)}, u32[]{:S(2)}) copy-start(f32[32,128]{1,0:T(8,128)} %param.14) | copy-start | bytes 49156
  62.0 49.8 %collective-permute-start.4 = (f32[16,32,128]{2,0,1:T(8,128)}, f32[16,32,128]{2,0,1:T(8,128)S(1)}, u32[]{:S(2)}, u32[]{:S(2)}) collective-permute-start(f32[16,32,128]{2,0,1:T(8,128)} %get-tuple-element.18), channel_id=1, source_target_pairs={{8,0},{12,4},{16,8},{20,12},{24,16},{28,20},{0,24},{4,28},{9,1},{1... | collective-permute-start | bytes 786440 | tf_op jit(solution)/shard_map/ppermute | solution.py:19
  62.0 49.8 %collective-permute-start.7 = (f32[16,32,128]{2,0,1:T(8,128)}, f32[16,32,128]{2,0,1:T(8,128)S(1)}, u32[]{:S(2)}, u32[]{:S(2)}) collective-permute-start(f32[16,32,128]{2,0,1:T(8,128)} %get-tuple-element.19), channel_id=1, source_target_pairs={{24,0},{28,4},{0,8},{4,12},{8,16},{12,20},{16,24},{20,28},{25,1},{... | collective-permute-start | bytes 786440 | tf_op jit(solution)/shard_map/ppermute | solution.py:19
  64.0 47.7 %collective-permute-start.6 = (f32[16,32,128]{2,0,1:T(8,128)S(1)}, f32[16,32,128]{2,0,1:T(8,128)S(1)}, u32[]{:S(2)}, u32[]{:S(2)}) collective-permute-start(f32[16,32,128]{2,0,1:T(8,128)S(1)} %get-tuple-element.20), channel_id=1, source_target_pairs={{28,0},{0,4},{4,8},{8,12},{12,16},{16,20},{20,24},{24,28},{29,1},{... | collective-permute-start | bytes 786440 | tf_op jit(solution)/shard_map/ppermute | solution.py:19
  65.5 46.3 %collective-permute-start.5 = (f32[16,32,128]{2,0,1:T(8,128)S(1)}, f32[16,32,128]{2,0,1:T(8,128)S(1)}, u32[]{:S(2)}, u32[]{:S(2)}) collective-permute-start(f32[16,32,128]{2,0,1:T(8,128)S(1)} %get-tuple-element.21), channel_id=1, source_target_pairs={{4,0},{8,4},{12,8},{16,12},{20,16},{24,20},{28,24},{0,28},{5,1},{9... | collective-permute-start | bytes 786440 | tf_op jit(solution)/shard_map/ppermute | solution.py:19
where the time goes:
time: 113 us
  blocking collectives  60.6 us (54%)
  matrix products  27.5 us (24%)
  starting transfers between devices  16.6 us (15%)
  other arithmetic  3.56 us (3%)
  local copies, waits for them, and re-layouts  2.92 us (3%)
  between operations  1.42 us (1%)
    psum x1, blocking collectives, per_device(): grad = lax.psum(grad_local, 'node') * (1.0 / math.sqrt(node_total))  40.8 us
    ppermute x8, starting transfers between devices, passed_along(): return lax.ppermute(block, axis, route)  16.6 us
    all_gather x1, blocking collectives, per_device(): slope_all = lax.all_gather(slope_grad, 'feat', axis=1, tiled=True)  7.46 us
    all_gather x1, blocking collectives, per_device(): lax.all_gather(aggregate, 'feat', axis=1, tiled=True)  7.25 us
    dot_general x1, matrix products, per_device(): jnp.einsum('tfk,tjk->tfj', sources, tile_values, preferred_element_type=j...  7.25 us
    dot_general x1, matrix products, per_device(): jnp.einsum('tfj,tjk->tfk', back_sources, tile_values, preferred_element_t...  7.21 us
    all_gather x1, blocking collectives, per_device(): lax.all_gather(weight_half, 'feat', axis=0, tiled=True)  5.18 us
    dot_general x1, matrix products, per_device(): jnp.einsum('ts,tfk->sfk', add_source, back_terms, precision=lax.Precision...  4.89 us
  transfers between devices with their start and end apart: 8, of which 0 were waited for; matrix products, arithmetic and copies ran while one was open for 5% of the time, Pallas kernels for 0%

commit v1 on v0

--- a/solution.py
+++ b/solution.py
@@ -11,6 +11,11 @@
 first_fix = 1.0 - 0.9**10
 second_fix = 1.0 - 0.999**10
 adam_eps = 1e-08
+
+
+def gather_and_add(x, axis):
+    pieces = lax.all_gather(x, axis)
+    return jnp.sum(pieces, axis=0)
 
 
 def passed_along(block, axis, distance):
@@ -86,7 +91,7 @@
     slope_all = lax.all_gather(slope_grad, "feat", axis=1, tiled=True)
     node_total = cycle_size * blocks * tile_size
     grad_local = jnp.einsum("bij,boj->io", aggregate, slope_all, preferred_element_type=jnp.float32)
-    grad = lax.psum(grad_local, "node") * (1.0 / math.sqrt(node_total))
+    grad = gather_and_add(grad_local, "node") * (1.0 / math.sqrt(node_total))
     back_rows = jnp.einsum(
         "io,boj->bij", weight_half, slope_all, preferred_element_type=jnp.float32
     ).astype(jnp.bfloat16)

time: 113 us -> 109 us (0.965)
  blocking collectives: 60.6 us -> 57.8 us
    psum x1 -> x0, blocking collectives: 40.8 us -> none  [per_device(): grad = lax.psum(grad_local, 'node') * (1.0 / math.sqrt(node_total))]
    all_gather x0 -> x1, blocking collectives: none -> 37.9 us  [gather_and_add(): pieces = lax.all_gather(x, axis)]
  transfers between devices with their start and end apart: 8 -> 8, of which waited for: 0 -> 0; matrix products, arithmetic and copies ran while one was open for 5% -> 4% of each run, Pallas kernels for 0% -> 0%
where the time goes in v1:
time: 109 us
  blocking collectives  57.8 us (53%)
  matrix products  26.9 us (25%)
  starting transfers between devices  16.6 us (15%)
  other arithmetic  3.59 us (3%)
  local copies, waits for them, and re-layouts  2.1 us (2%)
  between operations  1.44 us (1%)
    all_gather x1, blocking collectives, gather_and_add(): pieces = lax.all_gather(x, axis)  37.9 us
    ppermute x8, starting transfers between devices, passed_along(): return lax.ppermute(block, axis, route)  16.6 us
    all_gather x1, blocking collectives, per_device(): slope_all = lax.all_gather(slope_grad, 'feat', axis=1, tiled=True)  7.46 us
    all_gather x1, blocking collectives, per_device(): lax.all_gather(aggregate, 'feat', axis=1, tiled=True)  7.25 us
    dot_general x1, matrix products, per_device(): jnp.einsum('tfk,tjk->tfj', sources, tile_values, preferred_element_type=j...  7.25 us
    dot_general x1, matrix products, per_device(): jnp.einsum('tfj,tjk->tfk', back_sources, tile_values, preferred_element_t...  7.21 us
    all_gather x1, blocking collectives, per_device(): lax.all_gather(weight_half, 'feat', axis=0, tiled=True)  5.18 us
    dot_general x1, matrix products, per_device(): jnp.einsum('ts,tfk->sfk', add_source, back_terms, precision=lax.Precision...  4.89 us
  transfers between devices with their start and end apart: 8, of which 0 were waited for; matrix products, arithmetic and copies ran while one was open for 4% of the time, Pallas kernels for 0%

profile of v1, /device:TPU:0, one launch (start us, length us, event | category | flops | bytes accessed | tf_op | source)
XLA Modules:
  0.0 108.5 jit_solution(9557402522557386790)
XLA Ops:
  0.6 6.0 %collective-permute-start.2 = (bf16[16,32,128]{2,1,0:T(8,128)(2,1)}, bf16[16,32,128]{2,1,0:T(8,128)(2,1)S(1)}, u32[]{:S(2)}, u32[]{:S(2)}) collective-permute-start(bf16[16,32,128]{2,1,0:T(8,128)(2,1)} %param.9), channel_id=1, source_target_pairs={{4,0},{8,4},{12,8},{16,12},{20,16},{24,20},{28,24},{0,28},{5,1},{9... | collective-permute-start | bytes 393224 | tf_op jit(solution)/shard_map/ppermute | solution.py:24
  6.7 0.0 collective-permute-start.1
  6.7 3.8 %collective-permute-start.3 = (bf16[16,32,128]{2,1,0:T(8,128)(2,1)}, bf16[16,32,128]{2,1,0:T(8,128)(2,1)S(1)}, u32[]{:S(2)}, u32[]{:S(2)}) collective-permute-start(bf16[16,32,128]{2,1,0:T(8,128)(2,1)} %param.9), channel_id=1, source_target_pairs={{8,0},{12,4},{16,8},{20,12},{24,16},{28,20},{0,24},{4,28},{9,1},{1... | collective-permute-start | bytes 393224 | tf_op jit(solution)/shard_map/ppermute | solution.py:24
  10.5 0.7 fusion.41
  11.2 0.7 broadcast_subtract_fusion
  12.5 0.7 convert_element_type.38
  13.3 5.2 %all_gather.15 = bf16[128,128]{1,0:T(8,128)(2,1)S(1)} all-gather(bf16[32,128]{1,0:T(8,128)(2,1)S(1)} %convert_element_type.38), channel_id=1, replica_groups=mesh['node'=8,'feat'=4] {'feat'}, dimensions={0}, use_global_device_ids=true | all-gather | bytes 40960 | tf_op jit(solution)/shard_map/all_gather | solution.py:82
  18.4 0.0 collective-permute-done
  18.5 0.0 collective-permute-done.1
  18.5 0.9 constant_dynamic-update-slice_fusion.2
  19.5 0.8 fusion.10
  20.3 7.2 %fusion.4 = f32[256,32,128]{2,1,0:T(8,128)S(1)} fusion(bf16[256,128,128]{2,1,0:T(8,128)(2,1)} %param.10, bf16[256,32,128]{2,0,1:T(8,128)(2,1)S(1)} %fusion.10), kind=kOutput, calls=%fused_computation.6 | convolution fusion | flops 268435456 | bytes 14680064 | tf_op jit(solution)/shard_map/tfk,tjk->tfj/dot_general | solution.py:74
  27.5 4.4 %fusion.7 = bf16[16,32,128]{2,0,1:T(8,128)(2,1)S(1)} fusion(f32[256,32,128]{2,1,0:T(8,128)S(1)} %fusion.4, f32[256]{0:T(256)S(1)} %compare_convert_fusion, s32[256]{0:T(256)S(1)} %broadcast_subtract_fusion), kind=kOutput, calls=%fused_computation.11 | convolution fusion | flops 201400320 | bytes 4327424 | tf_op jit(solution)/shard_map/tb,tfj->bfj/dot_general | solution.py:77
  31.9 7.3 %all_gather.16 = bf16[16,128,128]{2,0,1:T(8,128)(2,1)S(1)} all-gather(bf16[16,32,128]{2,0,1:T(8,128)(2,1)S(1)} %fusion.7), channel_id=1, replica_groups=mesh['node'=8,'feat'=4] {'feat'}, dimensions={1}, use_global_device_ids=true | all-gather | bytes 655360 | tf_op jit(solution)/shard_map/all_gather | solution.py:81
  39.1 1.1 fusion.16
  40.2 7.5 %all_gather.17 = bf16[16,128,128]{2,1,0:T(8,128)(2,1)S(1)} all-gather(bf16[16,32,128]{2,1,0:T(8,128)(2,1)S(1)} %get-tuple-element.22), channel_id=1, replica_groups=mesh['node'=8,'feat'=4] {'feat'}, dimensions={1}, use_global_device_ids=true | all-gather | bytes 655360 | tf_op jit(solution)/shard_map/all_gather | solution.py:91
  47.7 0.3 convolution_bitcast_fusion.1
  47.9 0.4 fusion.6
  48.3 0.2 copy.25
  48.5 0.7 fusion.34
  49.3 7.2 %fusion.5 = f32[256,32,128]{2,1,0:T(8,128)S(1)} fusion(bf16[256,128,128]{2,1,0:T(8,128)(2,1)} %param.10, bf16[256,32,128]{2,0,1:T(8,128)(2,1)S(1)} %fusion.34), kind=kOutput, calls=%fused_computation.7 | convolution fusion | flops 268435456 | bytes 14680064 | tf_op jit(solution)/shard_map/tfj,tjk->tfk/dot_general | solution.py:101
  56.5 4.9 %fusion = f32[80,32,128]{2,0,1:T(8,128)S(1)} fusion(f32[256,32,128]{2,1,0:T(8,128)S(1)} %fusion.5, f32[256]{0:T(256)S(1)} %compare_convert_fusion, s32[256]{0:T(256)S(1)} %fusion.41), kind=kOutput, calls=%fused_computation | convolution fusion | flops 1006673920 | bytes 5507072 | tf_op jit(solution)/shard_map/ts,tfk->sfk/dot_general | solution.py:104
  61.4 0.1 fusion.48
  61.5 0.1 collective-permute-start.4
  61.6 2.0 %collective-permute-start.7 = (f32[16,32,128]{2,0,1:T(8,128)S(1)}, f32[16,32,128]{2,0,1:T(8,128)S(1)}, u32[]{:S(2)}, u32[]{:S(2)}) collective-permute-start(f32[16,32,128]{2,0,1:T(8,128)S(1)} %get-tuple-element.19), channel_id=1, source_target_pairs={{24,0},{28,4},{0,8},{4,12},{8,16},{12,20},{16,24},{20,28},{25,1},{... | collective-permute-start | bytes 786440 | tf_op jit(solution)/shard_map/ppermute | solution.py:24
  63.6 1.5 %collective-permute-start.6 = (f32[16,32,128]{2,0,1:T(8,128)S(1)}, f32[16,32,128]{2,0,1:T(8,128)S(1)}, u32[]{:S(2)}, u32[]{:S(2)}) collective-permute-start(f32[16,32,128]{2,0,1:T(8,128)S(1)} %get-tuple-element.20), channel_id=1, source_target_pairs={{28,0},{0,4},{4,8},{8,12},{12,16},{16,20},{20,24},{24,28},{29,1},{... | collective-permute-start | bytes 786440 | tf_op jit(solution)/shard_map/ppermute | solution.py:24
  65.0 3.3 %collective-permute-start.5 = (f32[16,32,128]{2,0,1:T(8,128)S(1)}, f32[16,32,128]{2,0,1:T(8,128)S(1)}, u32[]{:S(2)}, u32[]{:S(2)}) collective-permute-start(f32[16,32,128]{2,0,1:T(8,128)S(1)} %get-tuple-element.21), channel_id=1, source_target_pairs={{4,0},{8,4},{12,8},{16,12},{20,16},{24,20},{28,24},{0,28},{5,1},{9... | collective-permute-start | bytes 786440 | tf_op jit(solution)/shard_map/ppermute | solution.py:24
  68.3 37.9 %all-gather = f32[256,128]{1,0:T(8,128)S(1)} all-gather(f32[32,128]{1,0:T(8,128)S(1)} %convolution_bitcast_fusion.1), channel_id=2, replica_groups=mesh['node'=8,'feat'=4] {'node'}, dimensions={0}, use_global_device_ids=true | all-gather | bytes 147456 | tf_op jit(solution)/shard_map/all_gather | solution.py:17
  106.2 1.4 %divide_subtract_fusion = (f32[32,128]{1,0:T(8,128)}, f32[32,128]{1,0:T(8,128)}, f32[32,128]{1,0:T(8,128)}) fusion(f32[32,128]{1,0:T(8,128)} %param.14, f32[32,128]{1,0:T(8,128)S(1)} %reduce_sum.9, f32[32,128]{1,0:T(8,128)} %param.15, f32[32,128]{1,0:T(8,128)} %param.16), kind=kLoop, calls=%fused_computation.39 | loop fusion | flops 53248 | bytes 114688 | tf_op jit(solution)/shard_map/sub | solution.py:112
  107.6 0.0 collective-permute-done.4
  107.7 0.1 fusion.19
  107.7 0.8 copy.21
  (14 shorter events, 0.1 us)
Async XLA Ops:
  0.6 18.8 %collective-permute-start.2 = (bf16[16,32,128]{2,1,0:T(8,128)(2,1)}, bf16[16,32,128]{2,1,0:T(8,128)(2,1)S(1)}, u32[]{:S(2)}, u32[]{:S(2)}) collective-permute-start(bf16[16,32,128]{2,1,0:T(8,128)(2,1)} %param.9), channel_id=1, source_target_pairs={{4,0},{8,4},{12,8},{16,12},{20,16},{24,20},{28,24},{0,28},{5,1},{9... | collective-permute-start | bytes 393224 | tf_op jit(solution)/shard_map/ppermute | solution.py:24
  6.7 11.8 %collective-permute-start.1 = (bf16[16,32,128]{2,1,0:T(8,128)(2,1)}, bf16[16,32,128]{2,1,0:T(8,128)(2,1)S(1)}, u32[]{:S(2)}, u32[]{:S(2)}) collective-permute-start(bf16[16,32,128]{2,1,0:T(8,128)(2,1)} %param.9), channel_id=1, source_target_pairs={{28,0},{0,4},{4,8},{8,12},{12,16},{16,20},{20,24},{24,28},{29,1},{... | collective-permute-start | bytes 393224 | tf_op jit(solution)/shard_map/ppermute | solution.py:24
  6.7 11.8 %collective-permute-start = (bf16[16,32,128]{2,1,0:T(8,128)(2,1)}, bf16[16,32,128]{2,1,0:T(8,128)(2,1)S(1)}, u32[]{:S(2)}, u32[]{:S(2)}) collective-permute-start(bf16[16,32,128]{2,1,0:T(8,128)(2,1)} %param.9), channel_id=1, source_target_pairs={{24,0},{28,4},{0,8},{4,12},{8,16},{12,20},{16,24},{20,28},{25,1},{... | collective-permute-start | bytes 393224 | tf_op jit(solution)/shard_map/ppermute | solution.py:24
  6.7 12.8 %collective-permute-start.3 = (bf16[16,32,128]{2,1,0:T(8,128)(2,1)}, bf16[16,32,128]{2,1,0:T(8,128)(2,1)S(1)}, u32[]{:S(2)}, u32[]{:S(2)}) collective-permute-start(bf16[16,32,128]{2,1,0:T(8,128)(2,1)} %param.9), channel_id=1, source_target_pairs={{8,0},{12,4},{16,8},{20,12},{24,16},{28,20},{0,24},{4,28},{9,1},{1... | collective-permute-start | bytes 393224 | tf_op jit(solution)/shard_map/ppermute | solution.py:24
  27.5 11.6 %copy-start = (bf16[16,32,128]{2,1,0:T(8,128)(2,1)S(1)}, bf16[16,32,128]{2,1,0:T(8,128)(2,1)}, u32[]{:S(2)}) copy-start(bf16[16,32,128]{2,1,0:T(8,128)(2,1)} %param.17) | copy-start | bytes 393220
  61.5 46.1 %collective-permute-start.4 = (f32[16,32,128]{2,0,1:T(8,128)S(1)}, f32[16,32,128]{2,0,1:T(8,128)S(1)}, u32[]{:S(2)}, u32[]{:S(2)}) collective-permute-start(f32[16,32,128]{2,0,1:T(8,128)S(1)} %get-tuple-element.18), channel_id=1, source_target_pairs={{8,0},{12,4},{16,8},{20,12},{24,16},{28,20},{0,24},{4,28},{9,1},{1... | collective-permute-start | bytes 786440 | tf_op jit(solution)/shard_map/ppermute | solution.py:24
  61.6 46.1 %collective-permute-start.7 = (f32[16,32,128]{2,0,1:T(8,128)S(1)}, f32[16,32,128]{2,0,1:T(8,128)S(1)}, u32[]{:S(2)}, u32[]{:S(2)}) collective-permute-start(f32[16,32,128]{2,0,1:T(8,128)S(1)} %get-tuple-element.19), channel_id=1, source_target_pairs={{24,0},{28,4},{0,8},{4,12},{8,16},{12,20},{16,24},{20,28},{25,1},{... | collective-permute-start | bytes 786440 | tf_op jit(solution)/shard_map/ppermute | solution.py:24
  63.6 44.1 %collective-permute-start.6 = (f32[16,32,128]{2,0,1:T(8,128)S(1)}, f32[16,32,128]{2,0,1:T(8,128)S(1)}, u32[]{:S(2)}, u32[]{:S(2)}) collective-permute-start(f32[16,32,128]{2,0,1:T(8,128)S(1)} %get-tuple-element.20), channel_id=1, source_target_pairs={{28,0},{0,4},{4,8},{8,12},{12,16},{16,20},{20,24},{24,28},{29,1},{... | collective-permute-start | bytes 786440 | tf_op jit(solution)/shard_map/ppermute | solution.py:24
  65.0 42.6 %collective-permute-start.5 = (f32[16,32,128]{2,0,1:T(8,128)S(1)}, f32[16,32,128]{2,0,1:T(8,128)S(1)}, u32[]{:S(2)}, u32[]{:S(2)}) collective-permute-start(f32[16,32,128]{2,0,1:T(8,128)S(1)} %get-tuple-element.21), channel_id=1, source_target_pairs={{4,0},{8,4},{12,8},{16,12},{20,16},{24,20},{28,24},{0,28},{5,1},{9... | collective-permute-start | bytes 786440 | tf_op jit(solution)/shard_map/ppermute | solution.py:24
